TPU v7x, 256 devices: a whole 4x4x8 slice. The times are simulated.
256 devices in a mesh: row: 16 (over z_lo, x), col: 16 (over y, z_hi, core).
Axes of the slice: x: 4, y: 4, z: 8 (z_hi: 2, z_lo: 4; z = z_hi * 4 + z_lo), core: 2. Of those that a mesh axis runs over, the one named last changes fastest.
Arguments:
- traces: bfloat16 [32768, 1024], P(('row', 'col'))
- alive: int32 [32768], P(('row', 'col')), may hold values 0 or 1
- pair_list: int32 [1024, 2], P(('row', 'col')), may hold values from -1 to 255, as said below
Outputs:
- correlations: bfloat16 [1024, 128, 65, 128], P(('row', 'col'))
Inputs may be any that keep to these rules, and one draw needn't show every extreme that they name: `pair_list`: slots p * 4 to (p + 1) * 4 - 1 belong to flat device p = r * 16 + c (r its row index, c its col index); they hold 1 to 4 live pairs first and then (-1, -1) pairs; in every draw some device has all 4 slots live. A live pair (a, b) of that device has a // 16 == r, b % 16 == c and b >= a.
All inputs are finite; a program needn't handle non-finite values. No bound on the sum of `alive` on one device may be relied on, other than what follows from the above.
Results may differ from a plain program's by a relative error of at most 0.0042.
Values may be sent and summed in bfloat16 or wider, within the bound.
No kernel may reach another device: no remote copies, remote signals or barrier semaphores. Data moves between devices by JAX's collectives and lax.ppermute only.
A program may use at most 128 MiB of HBM per device.

v0:
```python
import jax
import jax.numpy as jnp
from jax import lax
from jax.sharding import PartitionSpec as P

LAGS = 65


def whiten(traces, alive):
    samples = traces.astype(jnp.float32)
    centered = samples - jnp.mean(samples, axis=1, keepdims=True)
    power = jnp.mean(centered * centered, axis=1, keepdims=True)
    factor = alive.astype(jnp.float32)[:, None] / jnp.sqrt(power + 1e-05)
    return (centered * factor).astype(jnp.bfloat16)


def correlate(left_block, right_block):
    length = left_block.shape[1]
    width = left_block.shape[0]
    reach = (LAGS - 1) // 2
    padded = jnp.pad(right_block, ((0, 0), (reach, reach)))
    shifted = jnp.stack([padded[:, offset : offset + length] for offset in range(LAGS)], axis=0)
    shifted = shifted.reshape(LAGS * width, length)
    summed = lax.dot_general(
        left_block, shifted, (((1,), (1,)), ((), ())), preferred_element_type=jnp.float32
    )
    return (summed * (1.0 / length)).reshape(width, LAGS, width).astype(jnp.bfloat16)


def shards(traces, alive, pair_list):
    whitened = whiten(traces, alive)
    block = whitened.shape[0]
    slots = pair_list.shape[0]
    across = lax.axis_size("col")
    row_panel = lax.all_gather(whitened, "col", axis=0, tiled=True)
    row_first = lax.axis_index("row") * across
    row_place = jnp.maximum(pair_list[:, 0] - row_first, 0)
    col_place = jnp.maximum(pair_list[:, 1], 0) // across
    living = jnp.sum((pair_list[:, 0] >= 0).astype(jnp.int32))
    buffer = jnp.zeros((slots, block, LAGS, block), jnp.bfloat16)

    def left_of(slot):
        return lax.dynamic_slice_in_dim(row_panel, row_place[slot] * block, block, 0)

    col_panel = lax.all_gather(whitened, "row", axis=0, tiled=True)

    def one_slot(slot, result):
        right_block = lax.dynamic_slice_in_dim(col_panel, col_place[slot] * block, block, 0)
        return lax.dynamic_update_index_in_dim(
            result, correlate(left_of(slot), right_block), slot, 0
        )

    correlations = lax.fori_loop(0, living, one_slot, buffer)
    return correlations


def solution(mesh):
    in_specs = (P(("row", "col"), None), P(("row", "col")), P(("row", "col"), None))
    out_specs = P(("row", "col"), None, None, None)
    return jax.shard_map(shards, mesh=mesh, in_specs=in_specs, out_specs=out_specs, check_vma=False)
```

profile of v0, /device:TPU:26, one launch (start us, length us, event | category | flops | bytes accessed | tf_op | source)
XLA Modules:
  0.0 344.4 jit_solution(5478605442784317596)
XLA Ops:
  6.5 1.1 convert_reduce_fusion
  7.6 1.2 fusion.5
  8.8 0.7 rsqrt_multiply_fusion
  9.4 1.9 fusion.6
  11.4 0.7 all-gather.5.cloned.1.call-update
  12.1 0.7 bitcast_select_fusion
  12.8 1.3 maximum_bitcast_fusion
  14.1 76.7 %all-gather.3.cloned.1.call-done = bf16[2048,1024]{1,0:T(8,128)(2,1)} async-done(((bf16[128,1024]{1,0:T(8,128)(2,1)}), bf16[2048,1024]{1,0:T(8,128)(2,1)}) %all-gather.3.cloned.1.call-update) | async-done | bytes 4194320 | tf_op jit(solution)/shard_map/all_gather | solution.py:35
  90.8 85.1 %all-gather.5.cloned.1.call-done = bf16[2048,1024]{1,0:T(8,128)(2,1)} async-done(((bf16[128,1024]{1,0:T(8,128)(2,1)}), bf16[2048,1024]{1,0:T(8,128)(2,1)}) %all-gather.5.cloned.1.call-update) | async-done | bytes 4194320 | tf_op jit(solution)/shard_map/all_gather | solution.py:45
  176.0 5.6 %broadcast_in_dim.3.clone = bf16[4,128,65,128]{3,1,2,0:T(8,128)(2,1)} broadcast(bf16[]{:T(256)} %constant.65.clone.1), dimensions={} | broadcast | bytes 8519682 | tf_op jit(solution)/shard_map/broadcast_in_dim | solution.py:40
  181.6 156.0 %while.12 = (s32[]{:T(128)}, bf16[4,128,65,128]{3,1,2,0:T(8,128)(2,1)}, s32[]{:T(128)}, s32[4]{0:T(128)S(1)}, bf16[2048,1024]{1,0:T(8,128)(2,1)}, /*index=5*/s32...) while((s32[]{:T(128)}, ...), condition=%wide.region_4.5_spmd, body=%wide.region_3.4_spmd.sunk | while | flops 2183168000 | bytes 134971696 | solution.py:53
  182.2 0.6 dynamic_slice.37
  183.4 1.0 constant_dynamic-slice_fusion.2
  184.5 0.1 bitcast_dynamic-update-slice_fusion.131
  189.0 1.0 bitcast_dynamic-update-slice_fusion.162
  194.6 5.8 %copy-done = bf16[65,128,1024]{2,1,0:T(8,128)(2,1)} copy-done((bf16[65,128,1024]{2,1,0:T(8,128)(2,1)}, bf16[65,128,1024]{2,1,0:T(8,128)(2,1)S(1)}, u32[]{:S(2)}) %copy-start) | copy-done | bytes 17039384 | tf_op jit(solution)/shard_map/while
  200.4 0.6 dynamic_slice.38
  201.6 11.5 %fusion.14 = bf16[128,8320]{1,0:T(8,128)(2,1)S(1)} fusion(bf16[8320,1024]{1,0:T(8,128)(2,1)} %bitcast.281, bf16[2048,1024]{1,0:T(8,128)(2,1)} %get-tuple-element.186, s32[]{:T(128)S(6)} %select_n.33), kind=kOutput, calls=%fused_computation.1.clone.1 | convolution fusion | flops 2183168000 | bytes 19431428 | tf_op jit(solution)/shard_map/while/body/dot_general | solution.py:24
  213.2 2.4 copy.11
  215.6 3.3 copy.12
  218.9 1.5 constant_dynamic-update-slice_fusion.2
  221.1 0.6 dynamic_slice.37
  222.2 1.0 constant_dynamic-slice_fusion.2
  227.8 1.0 bitcast_dynamic-update-slice_fusion.162
  233.4 5.8 %copy-done = bf16[65,128,1024]{2,1,0:T(8,128)(2,1)} copy-done((bf16[65,128,1024]{2,1,0:T(8,128)(2,1)}, bf16[65,128,1024]{2,1,0:T(8,128)(2,1)S(1)}, u32[]{:S(2)}) %copy-start) | copy-done | bytes 17039384 | tf_op jit(solution)/shard_map/while
  239.3 0.6 dynamic_slice.38
  240.5 11.5 %fusion.14 = bf16[128,8320]{1,0:T(8,128)(2,1)S(1)} fusion(bf16[8320,1024]{1,0:T(8,128)(2,1)} %bitcast.281, bf16[2048,1024]{1,0:T(8,128)(2,1)} %get-tuple-element.186, s32[]{:T(128)S(6)} %select_n.33), kind=kOutput, calls=%fused_computation.1.clone.1 | convolution fusion | flops 2183168000 | bytes 19431428 | tf_op jit(solution)/shard_map/while/body/dot_general | solution.py:24
  252.0 2.4 copy.11
  254.5 3.3 copy.12
  257.8 1.5 constant_dynamic-update-slice_fusion.2
  259.9 0.6 dynamic_slice.37
  261.1 1.0 constant_dynamic-slice_fusion.2
  266.7 1.0 bitcast_dynamic-update-slice_fusion.162
  272.3 5.8 %copy-done = bf16[65,128,1024]{2,1,0:T(8,128)(2,1)} copy-done((bf16[65,128,1024]{2,1,0:T(8,128)(2,1)}, bf16[65,128,1024]{2,1,0:T(8,128)(2,1)S(1)}, u32[]{:S(2)}) %copy-start) | copy-done | bytes 17039384 | tf_op jit(solution)/shard_map/while
  278.1 0.6 dynamic_slice.38
  279.3 11.5 %fusion.14 = bf16[128,8320]{1,0:T(8,128)(2,1)S(1)} fusion(bf16[8320,1024]{1,0:T(8,128)(2,1)} %bitcast.281, bf16[2048,1024]{1,0:T(8,128)(2,1)} %get-tuple-element.186, s32[]{:T(128)S(6)} %select_n.33), kind=kOutput, calls=%fused_computation.1.clone.1 | convolution fusion | flops 2183168000 | bytes 19431428 | tf_op jit(solution)/shard_map/while/body/dot_general | solution.py:24
  290.9 2.4 copy.11
  293.3 3.3 copy.12
  296.6 1.5 constant_dynamic-update-slice_fusion.2
  298.8 0.6 dynamic_slice.37
  299.9 1.0 constant_dynamic-slice_fusion.2
  305.5 1.0 bitcast_dynamic-update-slice_fusion.162
  311.1 5.8 %copy-done = bf16[65,128,1024]{2,1,0:T(8,128)(2,1)} copy-done((bf16[65,128,1024]{2,1,0:T(8,128)(2,1)}, bf16[65,128,1024]{2,1,0:T(8,128)(2,1)S(1)}, u32[]{:S(2)}) %copy-start) | copy-done | bytes 17039384 | tf_op jit(solution)/shard_map/while
  317.0 0.6 dynamic_slice.38
  318.2 11.5 %fusion.14 = bf16[128,8320]{1,0:T(8,128)(2,1)S(1)} fusion(bf16[8320,1024]{1,0:T(8,128)(2,1)} %bitcast.281, bf16[2048,1024]{1,0:T(8,128)(2,1)} %get-tuple-element.186, s32[]{:T(128)S(6)} %select_n.33), kind=kOutput, calls=%fused_computation.1.clone.1 | convolution fusion | flops 2183168000 | bytes 19431428 | tf_op jit(solution)/shard_map/while/body/dot_general | solution.py:24
  329.7 2.4 copy.11
  332.2 3.3 copy.12
  335.5 1.5 constant_dynamic-update-slice_fusion.2
  (263 shorter events, 35.2 us)
Async XLA Ops:
  6.5 84.3 %all-gather.3.cloned.1.call-start = ((), (), s32[]{:S(2)}) async-start(), calls=%async_computation | async-start | bytes 4456448 | tf_op jit(solution)/shard_map/all_gather | solution.py:35
  11.3 164.6 %all-gather.5.cloned.1.call-start = ((), (), s32[]{:S(2)}) async-start(), calls=%async_computation.1 | async-start | bytes 4456448 | tf_op jit(solution)/shard_map/all_gather | solution.py:45
  194.6 5.8 %copy-start = (bf16[65,128,1024]{2,1,0:T(8,128)(2,1)}, bf16[65,128,1024]{2,1,0:T(8,128)(2,1)S(1)}, u32[]{:S(2)}) copy-start(bf16[65,128,1024]{2,1,0:T(8,128)(2,1)S(1)} %bitcast_dynamic-update-slice_fusion.194) | copy-start | bytes 51118084 | tf_op jit(solution)/shard_map/while
  233.4 5.8 %copy-start = (bf16[65,128,1024]{2,1,0:T(8,128)(2,1)}, bf16[65,128,1024]{2,1,0:T(8,128)(2,1)S(1)}, u32[]{:S(2)}) copy-start(bf16[65,128,1024]{2,1,0:T(8,128)(2,1)S(1)} %bitcast_dynamic-update-slice_fusion.194) | copy-start | bytes 51118084 | tf_op jit(solution)/shard_map/while
  272.3 5.8 %copy-start = (bf16[65,128,1024]{2,1,0:T(8,128)(2,1)}, bf16[65,128,1024]{2,1,0:T(8,128)(2,1)S(1)}, u32[]{:S(2)}) copy-start(bf16[65,128,1024]{2,1,0:T(8,128)(2,1)S(1)} %bitcast_dynamic-update-slice_fusion.194) | copy-start | bytes 51118084 | tf_op jit(solution)/shard_map/while
  311.1 5.8 %copy-start = (bf16[65,128,1024]{2,1,0:T(8,128)(2,1)}, bf16[65,128,1024]{2,1,0:T(8,128)(2,1)S(1)}, u32[]{:S(2)}) copy-start(bf16[65,128,1024]{2,1,0:T(8,128)(2,1)S(1)} %bitcast_dynamic-update-slice_fusion.194) | copy-start | bytes 51118084 | tf_op jit(solution)/shard_map/while
Sparse Core Ops, SparseCore 0:
  11.5 79.3 all-gather.2
  92.6 83.3 all-gather.4
where the time goes:
time: 345 us; the launch traced here: 344 us
  waiting for transfers between devices  163 us (47%)
  local copies, waits for them, and re-layouts  106 us (31%)
  matrix products  46.1 us (13%)
  between operations  13.4 us (4%)
  loops' own time  9.93 us (3%)
  other arithmetic  6.8 us (2%)
    all_gather x1, waiting for transfers between devices, shards(): col_panel = lax.all_gather(whitened, 'row', axis=0, tiled=True)  85.1 us
    all_gather x1, waiting for transfers between devices, shards(): row_panel = lax.all_gather(whitened, 'col', axis=0, tiled=True)  76.7 us
    while x264, local copies, waits for them, and re-layouts  61.9 us
    dot_general x4, matrix products, correlate(): lax.dot_general(left_block, shifted, (((1,), (1,)), ((), ())), preferred_...  46.1 us
    dynamic_update_slice x8, local copies, waits for them, and re-layouts, one_slot(): lax.dynamic_update_index_in_dim(result, correlate(left_of(slot), right_bl...  19.1 us
    another operation x1, loops' own time, shards(): correlations = lax.fori_loop(0, living, one_slot, buffer)  9.93 us
    convert_element_type x4, local copies, waits for them, and re-layouts, correlate(): (summed * (1.0 / length)).reshape(width, LAGS, width).astype(jnp.bfloat16)  9.8 us
  transfers between devices with their start and end apart: 2, of which 2 were waited for; matrix products, arithmetic and copies ran while one was open for 1% of the time, Pallas kernels for 0%

commit v1 on v0

v1 whole, which is shorter than its diff:
```python
import jax
import jax.numpy as jnp
from jax import lax
from jax.experimental import pallas as pl
from jax.experimental.pallas import tpu as pltpu
from jax.sharding import PartitionSpec as P

LAGS = 65
REACH = (LAGS - 1) // 2
PAD = 64


def whiten(traces, alive):
    samples = traces.astype(jnp.float32)
    centered = samples - jnp.mean(samples, axis=1, keepdims=True)
    power = jnp.mean(centered * centered, axis=1, keepdims=True)
    factor = alive.astype(jnp.float32)[:, None] / jnp.sqrt(power + 1e-05)
    return (centered * factor).astype(jnp.bfloat16)


def correlate_kernel(live_ref, l_ref, r_ref, o_ref):
    slot = pl.program_id(0)
    length = l_ref.shape[2]

    @pl.when(live_ref[slot] > 0)
    def _():
        left = l_ref[0]
        for k in range(LAGS):
            shifted = r_ref[0, :, pl.ds(PAD - REACH + k, length)]
            summed = lax.dot_general(
                left, shifted, (((1,), (1,)), ((), ())), preferred_element_type=jnp.float32
            )
            o_ref[0, k] = (summed * (1.0 / length)).astype(o_ref.dtype)

    @pl.when(live_ref[slot] <= 0)
    def _():
        o_ref[...] = jnp.zeros(o_ref.shape, o_ref.dtype)


def correlate_all(live, left, right):
    slots, width, length = left.shape
    padded = jnp.pad(right, ((0, 0), (0, 0), (PAD, PAD)))
    out = pl.pallas_call(
        correlate_kernel,
        grid_spec=pltpu.PrefetchScalarGridSpec(
            num_scalar_prefetch=1,
            grid=(slots,),
            in_specs=[
                pl.BlockSpec((1, width, length), lambda s, lv: (s, 0, 0)),
                pl.BlockSpec((1, width, length + 2 * PAD), lambda s, lv: (s, 0, 0)),
            ],
            out_specs=pl.BlockSpec((1, LAGS, width, width), lambda s, lv: (s, 0, 0, 0)),
        ),
        out_shape=jax.ShapeDtypeStruct((slots, LAGS, width, width), jnp.bfloat16),
        compiler_params=pltpu.CompilerParams(vmem_limit_bytes=48 * 1024 * 1024),
    )(live, left, padded)
    return jnp.transpose(out, (0, 2, 1, 3))


def shards(traces, alive, pair_list):
    whitened = whiten(traces, alive)
    block = whitened.shape[0]
    across = lax.axis_size("col")
    row_panel = lax.all_gather(whitened, "col", axis=0, tiled=True)
    col_panel = lax.all_gather(whitened, "row", axis=0, tiled=True)
    row_first = lax.axis_index("row") * across
    row_place = jnp.clip(pair_list[:, 0] - row_first, 0, across - 1)
    col_place = jnp.maximum(pair_list[:, 1], 0) // across
    live = (pair_list[:, 0] >= 0).astype(jnp.int32)
    left = jnp.stack(
        [lax.dynamic_slice_in_dim(row_panel, row_place[s] * block, block, 0) for s in range(pair_list.shape[0])]
    )
    right = jnp.stack(
        [lax.dynamic_slice_in_dim(col_panel, col_place[s] * block, block, 0) for s in range(pair_list.shape[0])]
    )
    return correlate_all(live, left, right)


def solution(mesh):
    in_specs = (P(("row", "col"), None), P(("row", "col")), P(("row", "col"), None))
    out_specs = P(("row", "col"), None, None, None)
    return jax.shard_map(shards, mesh=mesh, in_specs=in_specs, out_specs=out_specs, check_vma=False)
```

time: 345 us -> 209 us (0.61)
  the two profiles are of different devices: /device:TPU:26 before, /device:TPU:16 now
where the time goes in v1:
time: 209 us; the launch traced here: 208 us
  waiting for transfers between devices  154 us (74%)
  Pallas kernels  24.2 us (12%)
  between operations  18.6 us (9%)
  other arithmetic  7.62 us (4%)
  local copies, waits for them, and re-layouts  3.82 us (2%)
    all_gather x1, waiting for transfers between devices, shards(): col_panel = lax.all_gather(whitened, 'row', axis=0, tiled=True)  84.4 us
    all_gather x1, waiting for transfers between devices, shards(): row_panel = lax.all_gather(whitened, 'col', axis=0, tiled=True)  69.1 us
    pallas_call x1, Pallas kernels, correlate_all(): pl.pallas_call(correlate_kernel, grid_spec=pltpu.PrefetchScalarGridSpec(n...  24.2 us
  transfers between devices with their start and end apart: 2, of which 2 were waited for; matrix products, arithmetic and copies ran while one was open for 2% of the time, Pallas kernels for 0%

profile of v1, /device:TPU:16, one launch (start us, length us, event | category | flops | bytes accessed | tf_op | source)
XLA Modules:
  0.0 208.5 jit_solution(1177283213348913498)
XLA Ops:
  6.5 0.0 all-gather.3.cloned.1.call-start
  6.5 1.1 convert_reduce_fusion
  7.6 1.2 fusion.6
  8.8 0.7 rsqrt_multiply_fusion
  9.4 1.9 fusion.7
  11.3 0.0 all-gather.3.cloned.1.call-update
  11.3 0.0 all-gather.5.cloned.1.call-start
  11.4 0.7 all-gather.5.cloned.1.call-update
  12.1 0.7 bitcast_select_fusion
  12.8 0.6 fusion.9
  16.0 0.7 subtract_clamp_fusion
  16.7 0.7 fusion.10
  20.0 0.7 fusion.8.live_ref
  20.6 69.1 %all-gather.3.cloned.1.call-done = bf16[2048,1024]{1,0:T(8,128)(2,1)} async-done(((bf16[128,1024]{1,0:T(8,128)(2,1)}), bf16[2048,1024]{1,0:T(8,128)(2,1)}) %all-gather.3.cloned.1.call-update) | async-done | bytes 4194320 | tf_op jit(solution)/shard_map/all_gather | solution.py:64
  89.7 1.3 dynamic-slice_bitcast_fusion.7
  91.0 0.1 pad_maximum_fusion.l_ref
  91.1 84.4 %all-gather.5.cloned.1.call-done = bf16[2048,1024]{1,0:T(8,128)(2,1)} async-done(((bf16[128,1024]{1,0:T(8,128)(2,1)}), bf16[2048,1024]{1,0:T(8,128)(2,1)}) %all-gather.5.cloned.1.call-update) | async-done | bytes 4194320 | tf_op jit(solution)/shard_map/all_gather | solution.py:65
  175.6 1.3 dynamic-slice_bitcast_fusion.3
  176.8 0.7 select_maximum_fusion.r_ref
  177.5 24.2 %shard_map.37 = bf16[4,65,128,128]{3,2,1,0:T(8,128)(2,1)} custom-call(s32[4]{0:T(128)S(1)} %fusion.8.live_ref, bf16[4,128,1024]{2,1,0:T(8,128)(2,1)S(1)} %pad_maximum_fusion.l_ref, bf16[4,128,1152]{2,1,0:T(8,128)(2,1)S(1)} %select_maximum_fusion.r_ref), custom_call_target="tpu_custom_call" | custom-call | tf_op jit(solution)/shard_map/pallas_call | solution.py:43
  (1 shorter events, 0.0 us)
Async XLA Ops:
  6.5 83.2 %all-gather.3.cloned.1.call-start = ((), (), s32[]{:S(2)}) async-start(), calls=%async_computation | async-start | bytes 4456448 | tf_op jit(solution)/shard_map/all_gather | solution.py:64
  11.3 164.2 %all-gather.5.cloned.1.call-start = ((), (), s32[]{:S(2)}) async-start(), calls=%async_computation.1 | async-start | bytes 4456448 | tf_op jit(solution)/shard_map/all_gather | solution.py:65
Sparse Core Ops, SparseCore 0:
  11.5 78.2 all-gather.2
  91.5 83.9 all-gather.4

commit v2 on v1

--- a/solution.py
+++ b/solution.py
@@ -8,6 +8,7 @@
 LAGS = 65
 REACH = (LAGS - 1) // 2
 PAD = 64
+META = 128
 
 
 def whiten(traces, alive):
@@ -57,22 +58,30 @@
     return jnp.transpose(out, (0, 2, 1, 3))
 
 
+def fetch_blocks(whitened, wanted, axis):
+    n = lax.axis_size(axis)
+    block, length = whitened.shape
+    piece = block // n
+    slots = wanted.shape[0]
+    meta = jnp.zeros((piece, META), whitened.dtype).at[0, :slots].set(wanted.astype(whitened.dtype))
+    pieces = jnp.concatenate(
+        [whitened.reshape(n, piece, length), jnp.broadcast_to(meta, (n, piece, META))], axis=2
+    )
+    spread = lax.all_to_all(pieces, axis, 0, 0, tiled=True)
+    asked = spread[:, 0, length:length + slots].astype(jnp.int32)
+    chosen = jnp.take(spread[:, :, :length], asked, axis=0)
+    arrived = lax.all_to_all(chosen, axis, 0, 0, tiled=True)
+    return jnp.transpose(arrived, (1, 0, 2, 3)).reshape(slots, block, length)
+
+
 def shards(traces, alive, pair_list):
     whitened = whiten(traces, alive)
-    block = whitened.shape[0]
     across = lax.axis_size("col")
-    row_panel = lax.all_gather(whitened, "col", axis=0, tiled=True)
-    col_panel = lax.all_gather(whitened, "row", axis=0, tiled=True)
-    row_first = lax.axis_index("row") * across
-    row_place = jnp.clip(pair_list[:, 0] - row_first, 0, across - 1)
-    col_place = jnp.maximum(pair_list[:, 1], 0) // across
+    first = jnp.maximum(pair_list[:, 0], 0)
+    second = jnp.maximum(pair_list[:, 1], 0)
     live = (pair_list[:, 0] >= 0).astype(jnp.int32)
-    left = jnp.stack(
-        [lax.dynamic_slice_in_dim(row_panel, row_place[s] * block, block, 0) for s in range(pair_list.shape[0])]
-    )
-    right = jnp.stack(
-        [lax.dynamic_slice_in_dim(col_panel, col_place[s] * block, block, 0) for s in range(pair_list.shape[0])]
-    )
+    left = fetch_blocks(whitened, first % across, "col")
+    right = fetch_blocks(whitened, second // across, "row")
     return correlate_all(live, left, right)
 
 

time: 209 us -> 137 us (0.66)
  the two profiles are of different devices: /device:TPU:16 before, /device:TPU:35 now
where the time goes in v2:
time: 137 us; the launch traced here: 136 us
  waiting for transfers between devices  64.1 us (47%)
  Pallas kernels  24.2 us (18%)
  starting transfers between devices  21.8 us (16%)
  blocking collectives  14.9 us (11%)
  other arithmetic  7.93 us (6%)
  local copies, waits for them, and re-layouts  3 us (2%)
    all_to_all x2, waiting for transfers between devices, fetch_blocks(): arrived = lax.all_to_all(chosen, axis, 0, 0, tiled=True)  51.8 us
    pallas_call x1, Pallas kernels, correlate_all(): pl.pallas_call(correlate_kernel, grid_spec=pltpu.PrefetchScalarGridSpec(n...  24.2 us
    all_to_all x1, blocking collectives, fetch_blocks(): spread = lax.all_to_all(pieces, axis, 0, 0, tiled=True)  14.9 us
    all_to_all x1, waiting for transfers between devices, fetch_blocks(): spread = lax.all_to_all(pieces, axis, 0, 0, tiled=True)  12.3 us
    all_to_all x1, starting transfers between devices, fetch_blocks(): spread = lax.all_to_all(pieces, axis, 0, 0, tiled=True)  11.2 us
    all_to_all x2, starting transfers between devices, fetch_blocks(): arrived = lax.all_to_all(chosen, axis, 0, 0, tiled=True)  10.6 us
  transfers between devices with their start and end apart: 3, of which 3 were waited for; matrix products, arithmetic and copies ran while one was open for 4% of the time, Pallas kernels for 0%

profile of v2, /device:TPU:35, one launch (start us, length us, event | category | flops | bytes accessed | tf_op | source)
XLA Modules:
  0.0 136.1 jit_solution(11456221237657152638)
XLA Ops:
  0.0 0.0 copy-start
  0.0 1.1 convert_reduce_fusion
  1.1 1.2 fusion.2
  2.3 0.8 fusion.7
  3.1 0.7 rsqrt_multiply_fusion
  3.7 1.2 fusion.4
  4.9 0.8 pad_maximum_fusion.1
  5.7 14.9 %all_to_all.20 = bf16[16,8,1152]{2,1,0:T(8,128)(2,1)S(1)} all-to-all(bf16[16,8,1152]{2,1,0:T(8,128)(2,1)S(1)} %get-tuple-element.30), channel_id=1, replica_groups=mesh['row'=16,'col'=16] {'row'}, dimensions={0} | all-to-all | bytes 589824 | tf_op jit(solution)/shard_map/all_to_all | solution.py:70
  20.6 11.2 %all-to-all-start = ((bf16[16,8,1152]{2,1,0:T(8,128)(2,1)}), bf16[16,8,1152]{2,1,0:T(8,128)(2,1)S(1)}, u32[]{:S(2)}, u32[]{:S(2)}) async-start(bf16[16,8,1152]{2,1,0:T(8,128)(2,1)} %get-tuple-element.31), calls=%async_computation | async-start | bytes 589824 | tf_op jit(solution)/shard_map/all_to_all | solution.py:70
  31.8 0.1 copy.45
  31.9 0.1 copy.41
  32.0 0.1 copy.42
  32.1 0.1 reshape.176
  32.3 0.6 gather_fusion.1
  32.9 1.1 broadcast_select_fusion
  34.0 12.3 %all-to-all-done = bf16[16,8,1152]{2,1,0:T(8,128)(2,1)S(1)} async-done(((bf16[16,8,1152]{2,1,0:T(8,128)(2,1)}), bf16[16,8,1152]{2,1,0:T(8,128)(2,1)S(1)}, u32[]{:S(2)}, u32[]{:S(2)}) %all-to-all-start) | async-done | bytes 294944 | tf_op jit(solution)/shard_map/all_to_all | solution.py:70
  46.3 5.1 %all-to-all-start.3 = ((bf16[16,4,8,1024]{3,2,1,0:T(8,128)(2,1)}), bf16[16,4,8,1024]{3,2,1,0:T(8,128)(2,1)S(1)}, u32[]{:S(2)}, u32[]{:S(2)}) async-start(bf16[16,4,8,1024]{3,2,1,0:T(8,128)(2,1)} %broadcast_select_fusion), calls=%async_computation.3 | async-start | bytes 2097152 | tf_op jit(solution)/shard_map/all_to_all | solution.py:73
  51.4 0.1 copy.44
  51.5 0.1 copy.37
  51.6 0.1 copy.38
  51.7 0.1 reshape.172
  51.8 0.6 gather_fusion
  52.5 1.1 broadcast_select_fusion.1
  53.6 21.4 %all-to-all-done.3 = bf16[16,4,8,1024]{3,2,1,0:T(8,128)(2,1)S(1)} async-done(((bf16[16,4,8,1024]{3,2,1,0:T(8,128)(2,1)}), bf16[16,4,8,1024]{3,2,1,0:T(8,128)(2,1)S(1)}, u32[]{:S(2)}, u32[]{:S(2)}) %all-to-all-start.3) | async-done | bytes 1048608 | tf_op jit(solution)/shard_map/all_to_all | solution.py:73
  75.0 5.5 %all-to-all-start.1 = ((bf16[16,4,8,1024]{3,2,1,0:T(8,128)(2,1)}), bf16[16,4,8,1024]{3,2,1,0:T(8,128)(2,1)S(1)}, u32[]{:S(2)}, u32[]{:S(2)}) async-start(bf16[16,4,8,1024]{3,2,1,0:T(8,128)(2,1)} %broadcast_select_fusion.1), calls=%async_computation.1 | async-start | bytes 2097152 | tf_op jit(solution)/shard_map/all_to_all | solution.py:73
  80.6 0.0 copy-done
  80.6 0.1 copy_bitcast_fusion
  80.7 0.8 pad.13.r_ref
  81.5 30.4 %all-to-all-done.1 = bf16[16,4,8,1024]{3,2,1,0:T(8,128)(2,1)S(1)} async-done(((bf16[16,4,8,1024]{3,2,1,0:T(8,128)(2,1)}), bf16[16,4,8,1024]{3,2,1,0:T(8,128)(2,1)S(1)}, u32[]{:S(2)}, u32[]{:S(2)}) %all-to-all-start.1) | async-done | bytes 1048608 | tf_op jit(solution)/shard_map/all_to_all | solution.py:73
  111.9 0.1 copy_bitcast_fusion.1.l_ref
  111.9 24.2 %shard_map.37 = bf16[4,65,128,128]{3,2,1,0:T(8,128)(2,1)} custom-call(s32[4]{0:T(128)S(1)} %fusion.5.live_ref, bf16[4,128,1024]{2,1,0:T(8,128)(2,1)S(1)} %copy_bitcast_fusion.1.l_ref, bf16[4,128,1152]{2,1,0:T(8,128)(2,1)S(1)} %pad.13.r_ref), custom_call_target="tpu_custom_call" | custom-call | tf_op jit(solution)/shard_map/pallas_call | solution.py:44
  (16 shorter events, 0.1 us)
Async XLA Ops:
  0.0 80.6 %copy-start = (s32[4,2]{0,1:T(2,128)S(1)}, s32[4,2]{0,1:T(2,128)}, u32[]{:S(2)}) copy-start(s32[4,2]{0,1:T(2,128)} %param.11) | copy-start | bytes 100
  20.6 25.7 %all-to-all-start = ((bf16[16,8,1152]{2,1,0:T(8,128)(2,1)}), bf16[16,8,1152]{2,1,0:T(8,128)(2,1)S(1)}, u32[]{:S(2)}, u32[]{:S(2)}) async-start(bf16[16,8,1152]{2,1,0:T(8,128)(2,1)} %get-tuple-element.31), calls=%async_computation | async-start | bytes 589824 | tf_op jit(solution)/shard_map/all_to_all | solution.py:70
  46.3 28.7 %all-to-all-start.3 = ((bf16[16,4,8,1024]{3,2,1,0:T(8,128)(2,1)}), bf16[16,4,8,1024]{3,2,1,0:T(8,128)(2,1)S(1)}, u32[]{:S(2)}, u32[]{:S(2)}) async-start(bf16[16,4,8,1024]{3,2,1,0:T(8,128)(2,1)} %broadcast_select_fusion), calls=%async_computation.3 | async-start | bytes 2097152 | tf_op jit(solution)/shard_map/all_to_all | solution.py:73
  75.0 36.8 %all-to-all-start.1 = ((bf16[16,4,8,1024]{3,2,1,0:T(8,128)(2,1)}), bf16[16,4,8,1024]{3,2,1,0:T(8,128)(2,1)S(1)}, u32[]{:S(2)}, u32[]{:S(2)}) async-start(bf16[16,4,8,1024]{3,2,1,0:T(8,128)(2,1)} %broadcast_select_fusion.1), calls=%async_computation.1 | async-start | bytes 2097152 | tf_op jit(solution)/shard_map/all_to_all | solution.py:73

commit v3 on v2

--- a/solution.py
+++ b/solution.py
@@ -27,10 +27,8 @@
     def _():
         left = l_ref[0]
         for k in range(LAGS):
-            shifted = r_ref[0, :, pl.ds(PAD - REACH + k, length)]
-            summed = lax.dot_general(
-                left, shifted, (((1,), (1,)), ((), ())), preferred_element_type=jnp.float32
-            )
+            shifted = r_ref[0, pl.ds(PAD - REACH + k, length), :].astype(jnp.bfloat16)
+            summed = jnp.dot(left, shifted, preferred_element_type=jnp.float32)
             o_ref[0, k] = (summed * (1.0 / length)).astype(o_ref.dtype)
 
     @pl.when(live_ref[slot] <= 0)
@@ -41,6 +39,7 @@
 def correlate_all(live, left, right):
     slots, width, length = left.shape
     padded = jnp.pad(right, ((0, 0), (0, 0), (PAD, PAD)))
+    padded = jnp.transpose(padded, (0, 2, 1)).astype(jnp.float32)
     out = pl.pallas_call(
         correlate_kernel,
         grid_spec=pltpu.PrefetchScalarGridSpec(
@@ -48,7 +47,7 @@
             grid=(slots,),
             in_specs=[
                 pl.BlockSpec((1, width, length), lambda s, lv: (s, 0, 0)),
-                pl.BlockSpec((1, width, length + 2 * PAD), lambda s, lv: (s, 0, 0)),
+                pl.BlockSpec((1, length + 2 * PAD, width), lambda s, lv: (s, 0, 0)),
             ],
             out_specs=pl.BlockSpec((1, LAGS, width, width), lambda s, lv: (s, 0, 0, 0)),
         ),

time: 137 us -> 134 us (0.978)
  the two profiles are of different devices: /device:TPU:35 before, /device:TPU:33 now
where the time goes in v3:
time: 134 us; the launch traced here: 133 us
  waiting for transfers between devices  62.8 us (47%)
  starting transfers between devices  20.9 us (16%)
  Pallas kernels  20.4 us (15%)
  blocking collectives  16.2 us (12%)
  other arithmetic  9.29 us (7%)
  local copies, waits for them, and re-layouts  3.52 us (3%)
    all_to_all x2, waiting for transfers between devices, fetch_blocks(): arrived = lax.all_to_all(chosen, axis, 0, 0, tiled=True)  50.5 us
    pallas_call x1, Pallas kernels, correlate_all(): pl.pallas_call(correlate_kernel, grid_spec=pltpu.PrefetchScalarGridSpec(n...  20.4 us
    all_to_all x1, blocking collectives, fetch_blocks(): spread = lax.all_to_all(pieces, axis, 0, 0, tiled=True)  16.2 us
    all_to_all x1, waiting for transfers between devices, fetch_blocks(): spread = lax.all_to_all(pieces, axis, 0, 0, tiled=True)  12.3 us
    all_to_all x1, starting transfers between devices, fetch_blocks(): spread = lax.all_to_all(pieces, axis, 0, 0, tiled=True)  11.2 us
    all_to_all x2, starting transfers between devices, fetch_blocks(): arrived = lax.all_to_all(chosen, axis, 0, 0, tiled=True)  9.69 us
  transfers between devices with their start and end apart: 3, of which 3 were waited for; matrix products, arithmetic and copies ran while one was open for 5% of the time, Pallas kernels for 0%

profile of v3, /device:TPU:33, one launch (start us, length us, event | category | flops | bytes accessed | tf_op | source)
XLA Modules:
  0.0 133.3 jit_solution(14730747109602407749)
XLA Ops:
  0.0 1.1 convert_reduce_fusion
  1.1 1.2 fusion.2
  2.2 0.8 fusion.7
  3.0 0.7 rsqrt_multiply_fusion
  3.7 1.2 fusion.4
  4.9 0.8 pad_maximum_fusion.1
  5.7 16.2 %all_to_all.20 = bf16[16,8,1152]{2,1,0:T(8,128)(2,1)S(1)} all-to-all(bf16[16,8,1152]{2,1,0:T(8,128)(2,1)S(1)} %get-tuple-element.30), channel_id=1, replica_groups=mesh['row'=16,'col'=16] {'row'}, dimensions={0} | all-to-all | bytes 589824 | tf_op jit(solution)/shard_map/all_to_all | solution.py:69
  21.8 11.2 %all-to-all-start = ((bf16[16,8,1152]{2,1,0:T(8,128)(2,1)}), bf16[16,8,1152]{2,1,0:T(8,128)(2,1)S(1)}, u32[]{:S(2)}, u32[]{:S(2)}) async-start(bf16[16,8,1152]{2,1,0:T(8,128)(2,1)} %get-tuple-element.31), calls=%async_computation | async-start | bytes 589824 | tf_op jit(solution)/shard_map/all_to_all | solution.py:69
  33.0 0.1 copy.49
  33.2 0.1 copy.44
  33.3 0.1 copy.45
  33.4 0.1 reshape.176
  33.5 0.6 gather_fusion.1
  34.1 1.1 broadcast_select_fusion
  35.2 12.3 %all-to-all-done = bf16[16,8,1152]{2,1,0:T(8,128)(2,1)S(1)} async-done(((bf16[16,8,1152]{2,1,0:T(8,128)(2,1)}), bf16[16,8,1152]{2,1,0:T(8,128)(2,1)S(1)}, u32[]{:S(2)}, u32[]{:S(2)}) %all-to-all-start) | async-done | bytes 294944 | tf_op jit(solution)/shard_map/all_to_all | solution.py:69
  47.6 3.9 %all-to-all-start.3 = ((bf16[16,4,8,1024]{3,2,1,0:T(8,128)(2,1)}), bf16[16,4,8,1024]{3,2,1,0:T(8,128)(2,1)S(1)}, u32[]{:S(2)}, u32[]{:S(2)}) async-start(bf16[16,4,8,1024]{3,2,1,0:T(8,128)(2,1)} %broadcast_select_fusion), calls=%async_computation.3 | async-start | bytes 2097152 | tf_op jit(solution)/shard_map/all_to_all | solution.py:72
  51.4 0.1 copy.48
  51.5 0.1 copy.40
  51.6 0.1 copy.41
  51.7 0.1 reshape.172
  51.9 0.6 gather_fusion
  52.5 0.0 copy-start
  52.5 1.1 broadcast_select_fusion.1
  53.6 22.3 %all-to-all-done.3 = bf16[16,4,8,1024]{3,2,1,0:T(8,128)(2,1)S(1)} async-done(((bf16[16,4,8,1024]{3,2,1,0:T(8,128)(2,1)}), bf16[16,4,8,1024]{3,2,1,0:T(8,128)(2,1)S(1)}, u32[]{:S(2)}, u32[]{:S(2)}) %all-to-all-start.3) | async-done | bytes 1048608 | tf_op jit(solution)/shard_map/all_to_all | solution.py:72
  76.0 5.8 %all-to-all-start.1 = ((bf16[16,4,8,1024]{3,2,1,0:T(8,128)(2,1)}), bf16[16,4,8,1024]{3,2,1,0:T(8,128)(2,1)S(1)}, u32[]{:S(2)}, u32[]{:S(2)}) async-start(bf16[16,4,8,1024]{3,2,1,0:T(8,128)(2,1)} %broadcast_select_fusion.1), calls=%async_computation.1 | async-start | bytes 2097152 | tf_op jit(solution)/shard_map/all_to_all | solution.py:72
  81.8 0.0 copy-done
  81.8 0.1 copy_bitcast_fusion
  81.9 1.3 copy.47
  83.2 1.4 %convert_bitcast_fusion.r_ref = f32[4,1152,128]{2,1,0:T(8,128)S(1)} fusion(bf16[4,128,1024]{1,2,0:T(8,128)(2,1)} %copy.47), kind=kLoop, calls=%fused_computation.2 | loop fusion | flops 589824 | bytes 3407872 | tf_op jit(solution)/shard_map/convert_element_type | solution.py:42
  84.6 28.2 %all-to-all-done.1 = bf16[16,4,8,1024]{3,2,1,0:T(8,128)(2,1)S(1)} async-done(((bf16[16,4,8,1024]{3,2,1,0:T(8,128)(2,1)}), bf16[16,4,8,1024]{3,2,1,0:T(8,128)(2,1)S(1)}, u32[]{:S(2)}, u32[]{:S(2)}) %all-to-all-start.1) | async-done | bytes 1048608 | tf_op jit(solution)/shard_map/all_to_all | solution.py:72
  112.8 0.1 copy_bitcast_fusion.1.l_ref
  112.9 20.4 %shard_map.37 = bf16[4,65,128,128]{3,2,1,0:T(8,128)(2,1)} custom-call(s32[4]{0:T(128)S(1)} %fusion.5.live_ref, bf16[4,128,1024]{2,1,0:T(8,128)(2,1)S(1)} %copy_bitcast_fusion.1.l_ref, f32[4,1152,128]{2,1,0:T(8,128)S(1)} %convert_bitcast_fusion.r_ref), custom_call_target="tpu_custom_call" | custom-call | tf_op jit(solution)/shard_map/pallas_call | solution.py:43
  (16 shorter events, 0.1 us)
Async XLA Ops:
  21.8 25.7 %all-to-all-start = ((bf16[16,8,1152]{2,1,0:T(8,128)(2,1)}), bf16[16,8,1152]{2,1,0:T(8,128)(2,1)S(1)}, u32[]{:S(2)}, u32[]{:S(2)}) async-start(bf16[16,8,1152]{2,1,0:T(8,128)(2,1)} %get-tuple-element.31), calls=%async_computation | async-start | bytes 589824 | tf_op jit(solution)/shard_map/all_to_all | solution.py:69
  47.6 28.4 %all-to-all-start.3 = ((bf16[16,4,8,1024]{3,2,1,0:T(8,128)(2,1)}), bf16[16,4,8,1024]{3,2,1,0:T(8,128)(2,1)S(1)}, u32[]{:S(2)}, u32[]{:S(2)}) async-start(bf16[16,4,8,1024]{3,2,1,0:T(8,128)(2,1)} %broadcast_select_fusion), calls=%async_computation.3 | async-start | bytes 2097152 | tf_op jit(solution)/shard_map/all_to_all | solution.py:72
  52.5 29.3 %copy-start = (s32[4,2]{0,1:T(2,128)S(1)}, s32[4,2]{0,1:T(2,128)}, u32[]{:S(2)}) copy-start(s32[4,2]{0,1:T(2,128)} %param.11) | copy-start | bytes 100
  76.0 36.8 %all-to-all-start.1 = ((bf16[16,4,8,1024]{3,2,1,0:T(8,128)(2,1)}), bf16[16,4,8,1024]{3,2,1,0:T(8,128)(2,1)S(1)}, u32[]{:S(2)}, u32[]{:S(2)}) async-start(bf16[16,4,8,1024]{3,2,1,0:T(8,128)(2,1)} %broadcast_select_fusion.1), calls=%async_computation.1 | async-start | bytes 2097152 | tf_op jit(solution)/shard_map/all_to_all | solution.py:72

commit v4 on v3

--- a/solution.py
+++ b/solution.py
@@ -8,6 +8,7 @@
 LAGS = 65
 REACH = (LAGS - 1) // 2
 PAD = 64
+PAIR = 2
 META = 128
 
 
@@ -26,10 +27,16 @@
     @pl.when(live_ref[slot] > 0)
     def _():
         left = l_ref[0]
-        for k in range(LAGS):
-            shifted = r_ref[0, pl.ds(PAD - REACH + k, length), :].astype(jnp.bfloat16)
+        width = o_ref.shape[3]
+        for first in range(0, LAGS, PAIR):
+            lags = range(first, min(first + PAIR, LAGS))
+            shifted = jnp.concatenate(
+                [r_ref[0, pl.ds(PAD - REACH + k, length), :].astype(jnp.bfloat16) for k in lags], axis=1
+            )
             summed = jnp.dot(left, shifted, preferred_element_type=jnp.float32)
-            o_ref[0, k] = (summed * (1.0 / length)).astype(o_ref.dtype)
+            summed = (summed * (1.0 / length)).astype(o_ref.dtype)
+            for n, k in enumerate(lags):
+                o_ref[0, k] = summed[:, n * width:(n + 1) * width]
 
     @pl.when(live_ref[slot] <= 0)
     def _():

time: 134 us -> 125 us (0.933)
  Pallas kernels: 20.4 us -> 11.7 us
    pallas_call x1, Pallas kernels: 20.4 us -> 11.7 us  [correlate_all(): pl.pallas_call(correlate_kernel, grid_spec=pltpu.PrefetchScalarGridSpec(n...]
  transfers between devices with their start and end apart: 3 -> 3, of which waited for: 3 -> 3; matrix products, arithmetic and copies ran while one was open for 5% -> 6% of each run, Pallas kernels for 0% -> 0%
where the time goes in v4:
time: 125 us
  waiting for transfers between devices  62.8 us (50%)
  starting transfers between devices  20.9 us (17%)
  blocking collectives  16.2 us (13%)
  Pallas kernels  11.7 us (9%)
  other arithmetic  9.29 us (7%)
  local copies, waits for them, and re-layouts  3.52 us (3%)
    all_to_all x2, waiting for transfers between devices, fetch_blocks(): arrived = lax.all_to_all(chosen, axis, 0, 0, tiled=True)  50.5 us
    all_to_all x1, blocking collectives, fetch_blocks(): spread = lax.all_to_all(pieces, axis, 0, 0, tiled=True)  16.2 us
    all_to_all x1, waiting for transfers between devices, fetch_blocks(): spread = lax.all_to_all(pieces, axis, 0, 0, tiled=True)  12.3 us
    pallas_call x1, Pallas kernels, correlate_all(): pl.pallas_call(correlate_kernel, grid_spec=pltpu.PrefetchScalarGridSpec(n...  11.7 us
    all_to_all x1, starting transfers between devices, fetch_blocks(): spread = lax.all_to_all(pieces, axis, 0, 0, tiled=True)  11.2 us
    all_to_all x2, starting transfers between devices, fetch_blocks(): arrived = lax.all_to_all(chosen, axis, 0, 0, tiled=True)  9.69 us
  transfers between devices with their start and end apart: 3, of which 3 were waited for; matrix products, arithmetic and copies ran while one was open for 6% of the time, Pallas kernels for 0%

profile of v4, /device:TPU:33, one launch (start us, length us, event | category | flops | bytes accessed | tf_op | source)
XLA Modules:
  0.0 124.6 jit_solution(11165902162417455102)
XLA Ops:
  0.0 1.1 convert_reduce_fusion
  1.1 1.2 fusion.2
  2.2 0.8 fusion.7
  3.0 0.7 rsqrt_multiply_fusion
  3.7 1.2 fusion.4
  4.9 0.8 pad_maximum_fusion.1
  5.7 16.2 %all_to_all.20 = bf16[16,8,1152]{2,1,0:T(8,128)(2,1)S(1)} all-to-all(bf16[16,8,1152]{2,1,0:T(8,128)(2,1)S(1)} %get-tuple-element.30), channel_id=1, replica_groups=mesh['row'=16,'col'=16] {'row'}, dimensions={0} | all-to-all | bytes 589824 | tf_op jit(solution)/shard_map/all_to_all | solution.py:76
  21.8 11.2 %all-to-all-start = ((bf16[16,8,1152]{2,1,0:T(8,128)(2,1)}), bf16[16,8,1152]{2,1,0:T(8,128)(2,1)S(1)}, u32[]{:S(2)}, u32[]{:S(2)}) async-start(bf16[16,8,1152]{2,1,0:T(8,128)(2,1)} %get-tuple-element.31), calls=%async_computation | async-start | bytes 589824 | tf_op jit(solution)/shard_map/all_to_all | solution.py:76
  33.0 0.1 copy.49
  33.2 0.1 copy.44
  33.3 0.1 copy.45
  33.4 0.1 reshape.176
  33.5 0.6 gather_fusion.1
  34.1 1.1 broadcast_select_fusion
  35.2 12.3 %all-to-all-done = bf16[16,8,1152]{2,1,0:T(8,128)(2,1)S(1)} async-done(((bf16[16,8,1152]{2,1,0:T(8,128)(2,1)}), bf16[16,8,1152]{2,1,0:T(8,128)(2,1)S(1)}, u32[]{:S(2)}, u32[]{:S(2)}) %all-to-all-start) | async-done | bytes 294944 | tf_op jit(solution)/shard_map/all_to_all | solution.py:76
  47.6 3.9 %all-to-all-start.3 = ((bf16[16,4,8,1024]{3,2,1,0:T(8,128)(2,1)}), bf16[16,4,8,1024]{3,2,1,0:T(8,128)(2,1)S(1)}, u32[]{:S(2)}, u32[]{:S(2)}) async-start(bf16[16,4,8,1024]{3,2,1,0:T(8,128)(2,1)} %broadcast_select_fusion), calls=%async_computation.3 | async-start | bytes 2097152 | tf_op jit(solution)/shard_map/all_to_all | solution.py:79
  51.4 0.1 copy.48
  51.5 0.1 copy.40
  51.6 0.1 copy.41
  51.7 0.1 reshape.172
  51.9 0.6 gather_fusion
  52.5 0.0 copy-start
  52.5 1.1 broadcast_select_fusion.1
  53.6 22.3 %all-to-all-done.3 = bf16[16,4,8,1024]{3,2,1,0:T(8,128)(2,1)S(1)} async-done(((bf16[16,4,8,1024]{3,2,1,0:T(8,128)(2,1)}), bf16[16,4,8,1024]{3,2,1,0:T(8,128)(2,1)S(1)}, u32[]{:S(2)}, u32[]{:S(2)}) %all-to-all-start.3) | async-done | bytes 1048608 | tf_op jit(solution)/shard_map/all_to_all | solution.py:79
  76.0 5.8 %all-to-all-start.1 = ((bf16[16,4,8,1024]{3,2,1,0:T(8,128)(2,1)}), bf16[16,4,8,1024]{3,2,1,0:T(8,128)(2,1)S(1)}, u32[]{:S(2)}, u32[]{:S(2)}) async-start(bf16[16,4,8,1024]{3,2,1,0:T(8,128)(2,1)} %broadcast_select_fusion.1), calls=%async_computation.1 | async-start | bytes 2097152 | tf_op jit(solution)/shard_map/all_to_all | solution.py:79
  81.8 0.0 copy-done
  81.8 0.1 copy_bitcast_fusion
  81.9 1.3 %copy.47 = bf16[4,128,1024]{1,2,0:T(8,128)(2,1)} copy(bf16[4,128,1024]{2,1,0:T(8,128)(2,1)S(1)} %copy_bitcast_fusion) | data formatting | bytes 2097152 | tf_op jit(solution)/shard_map/reshape | solution.py:80
  83.2 1.4 %convert_bitcast_fusion.r_ref = f32[4,1152,128]{2,1,0:T(8,128)S(1)} fusion(bf16[4,128,1024]{1,2,0:T(8,128)(2,1)} %copy.47), kind=kLoop, calls=%fused_computation.2 | loop fusion | flops 589824 | bytes 3407872 | tf_op jit(solution)/shard_map/convert_element_type | solution.py:49
  84.6 28.2 %all-to-all-done.1 = bf16[16,4,8,1024]{3,2,1,0:T(8,128)(2,1)S(1)} async-done(((bf16[16,4,8,1024]{3,2,1,0:T(8,128)(2,1)}), bf16[16,4,8,1024]{3,2,1,0:T(8,128)(2,1)S(1)}, u32[]{:S(2)}, u32[]{:S(2)}) %all-to-all-start.1) | async-done | bytes 1048608 | tf_op jit(solution)/shard_map/all_to_all | solution.py:79
  112.8 0.1 copy_bitcast_fusion.1.l_ref
  112.9 11.7 %shard_map.37 = bf16[4,65,128,128]{3,2,1,0:T(8,128)(2,1)} custom-call(s32[4]{0:T(128)S(1)} %fusion.5.live_ref, bf16[4,128,1024]{2,1,0:T(8,128)(2,1)S(1)} %copy_bitcast_fusion.1.l_ref, f32[4,1152,128]{2,1,0:T(8,128)S(1)} %convert_bitcast_fusion.r_ref), custom_call_target="tpu_custom_call" | custom-call | tf_op jit(solution)/shard_map/pallas_call | solution.py:50
  (16 shorter events, 0.1 us)
Async XLA Ops:
  21.8 25.7 %all-to-all-start = ((bf16[16,8,1152]{2,1,0:T(8,128)(2,1)}), bf16[16,8,1152]{2,1,0:T(8,128)(2,1)S(1)}, u32[]{:S(2)}, u32[]{:S(2)}) async-start(bf16[16,8,1152]{2,1,0:T(8,128)(2,1)} %get-tuple-element.31), calls=%async_computation | async-start | bytes 589824 | tf_op jit(solution)/shard_map/all_to_all | solution.py:76
  47.6 28.4 %all-to-all-start.3 = ((bf16[16,4,8,1024]{3,2,1,0:T(8,128)(2,1)}), bf16[16,4,8,1024]{3,2,1,0:T(8,128)(2,1)S(1)}, u32[]{:S(2)}, u32[]{:S(2)}) async-start(bf16[16,4,8,1024]{3,2,1,0:T(8,128)(2,1)} %broadcast_select_fusion), calls=%async_computation.3 | async-start | bytes 2097152 | tf_op jit(solution)/shard_map/all_to_all | solution.py:79
  52.5 29.3 %copy-start = (s32[4,2]{0,1:T(2,128)S(1)}, s32[4,2]{0,1:T(2,128)}, u32[]{:S(2)}) copy-start(s32[4,2]{0,1:T(2,128)} %param.11) | copy-start | bytes 100
  76.0 36.8 %all-to-all-start.1 = ((bf16[16,4,8,1024]{3,2,1,0:T(8,128)(2,1)}), bf16[16,4,8,1024]{3,2,1,0:T(8,128)(2,1)S(1)}, u32[]{:S(2)}, u32[]{:S(2)}) async-start(bf16[16,4,8,1024]{3,2,1,0:T(8,128)(2,1)} %broadcast_select_fusion.1), calls=%async_computation.1 | async-start | bytes 2097152 | tf_op jit(solution)/shard_map/all_to_all | solution.py:79

commit v5 on v4

--- a/solution.py
+++ b/solution.py
@@ -64,30 +64,70 @@
     return jnp.transpose(out, (0, 2, 1, 3))
 
 
-def fetch_blocks(whitened, wanted, axis):
-    n = lax.axis_size(axis)
-    block, length = whitened.shape
-    piece = block // n
-    slots = wanted.shape[0]
-    meta = jnp.zeros((piece, META), whitened.dtype).at[0, :slots].set(wanted.astype(whitened.dtype))
-    pieces = jnp.concatenate(
-        [whitened.reshape(n, piece, length), jnp.broadcast_to(meta, (n, piece, META))], axis=2
-    )
+def prepare_kernel(pairs_ref, traces_ref, alive_ref, col_ref, row_ref):
+    pieces, piece, width = col_ref.shape
+    length = traces_ref.shape[1]
+    slots = pairs_ref.shape[0]
+    samples = traces_ref[...].astype(jnp.float32)
+    centered = samples - jnp.mean(samples, axis=1, keepdims=True)
+    power = jnp.mean(centered * centered, axis=1, keepdims=True)
+    channels = samples.shape[0]
+    alive = jnp.transpose(jnp.broadcast_to(alive_ref[...].astype(jnp.float32), (channels, channels)))[:, :1]
+    whitened = centered * (alive / jnp.sqrt(power + 1e-05))
+    sublane = lax.broadcasted_iota(jnp.int32, (piece, width - length), 0)
+    lane = lax.broadcasted_iota(jnp.int32, (piece, width - length), 1)
+    col_meta = jnp.zeros((piece, width - length), jnp.float32)
+    row_meta = jnp.zeros((piece, width - length), jnp.float32)
+    for s in range(slots):
+        at = (sublane == 0) & (lane == s)
+        col_meta = jnp.where(at, (jnp.maximum(pairs_ref[s, 0], 0) % pieces).astype(jnp.float32), col_meta)
+        row_meta = jnp.where(at, (jnp.maximum(pairs_ref[s, 1], 0) // pieces).astype(jnp.float32), row_meta)
+    for p in range(pieces):
+        rows = whitened[p * piece:(p + 1) * piece].astype(col_ref.dtype)
+        col_ref[p, :, :length] = rows
+        row_ref[p, :, :length] = rows
+        col_ref[p, :, length:] = col_meta.astype(col_ref.dtype)
+        row_ref[p, :, length:] = row_meta.astype(row_ref.dtype)
+
+
+def prepare(traces, alive, pair_list, pieces):
+    channels, length = traces.shape
+    shape = jax.ShapeDtypeStruct((pieces, channels // pieces, length + META), jnp.bfloat16)
+    return pl.pallas_call(
+        prepare_kernel,
+        grid_spec=pltpu.PrefetchScalarGridSpec(
+            num_scalar_prefetch=1,
+            grid=(),
+            in_specs=[
+                pl.BlockSpec((channels, length), lambda pr: (0, 0)),
+                pl.BlockSpec((1, channels), lambda pr: (0, 0)),
+            ],
+            out_specs=[
+                pl.BlockSpec(shape.shape, lambda pr: (0, 0, 0)),
+                pl.BlockSpec(shape.shape, lambda pr: (0, 0, 0)),
+            ],
+        ),
+        out_shape=[shape, shape],
+    )(pair_list, traces, alive.reshape(1, channels))
+
+
+def fetch_blocks(pieces, axis, slots):
+    n, piece, width = pieces.shape
+    length = width - META
     spread = lax.all_to_all(pieces, axis, 0, 0, tiled=True)
     asked = spread[:, 0, length:length + slots].astype(jnp.int32)
     chosen = jnp.take(spread[:, :, :length], asked, axis=0)
     arrived = lax.all_to_all(chosen, axis, 0, 0, tiled=True)
-    return jnp.transpose(arrived, (1, 0, 2, 3)).reshape(slots, block, length)
+    return jnp.transpose(arrived, (1, 0, 2, 3)).reshape(slots, n * piece, length)
 
 
 def shards(traces, alive, pair_list):
-    whitened = whiten(traces, alive)
     across = lax.axis_size("col")
-    first = jnp.maximum(pair_list[:, 0], 0)
-    second = jnp.maximum(pair_list[:, 1], 0)
+    slots = pair_list.shape[0]
+    col_pieces, row_pieces = prepare(traces, alive, pair_list, across)
     live = (pair_list[:, 0] >= 0).astype(jnp.int32)
-    left = fetch_blocks(whitened, first % across, "col")
-    right = fetch_blocks(whitened, second // across, "row")
+    left = fetch_blocks(col_pieces, "col", slots)
+    right = fetch_blocks(row_pieces, "row", slots)
     return correlate_all(live, left, right)
 
 

time: 125 us -> 124 us (level)
  the two profiles are of different devices: /device:TPU:33 before, /device:TPU:35 now
where the time goes in v5:
time: 124 us; the launch traced here: 122 us
  waiting for transfers between devices  62.3 us (50%)
  starting transfers between devices  21.8 us (18%)
  blocking collectives  15.2 us (12%)
  Pallas kernels  14.6 us (12%)
  local copies, waits for them, and re-layouts  4.81 us (4%)
  other arithmetic  3.71 us (3%)
    all_to_all x2, waiting for transfers between devices, fetch_blocks(): arrived = lax.all_to_all(chosen, axis, 0, 0, tiled=True)  49.9 us
    all_to_all x1, blocking collectives, fetch_blocks(): spread = lax.all_to_all(pieces, axis, 0, 0, tiled=True)  15.2 us
    all_to_all x1, waiting for transfers between devices, fetch_blocks(): spread = lax.all_to_all(pieces, axis, 0, 0, tiled=True)  12.3 us
    pallas_call x1, Pallas kernels, correlate_all(): pl.pallas_call(correlate_kernel, grid_spec=pltpu.PrefetchScalarGridSpec(n...  11.7 us
    all_to_all x1, starting transfers between devices, fetch_blocks(): spread = lax.all_to_all(pieces, axis, 0, 0, tiled=True)  11.2 us
    all_to_all x2, starting transfers between devices, fetch_blocks(): arrived = lax.all_to_all(chosen, axis, 0, 0, tiled=True)  10.6 us
    pallas_call x1, Pallas kernels, prepare(): pl.pallas_call(prepare_kernel, grid_spec=pltpu.PrefetchScalarGridSpec(num...  2.81 us
  transfers between devices with their start and end apart: 3, of which 3 were waited for; matrix products, arithmetic and copies ran while one was open for 6% of the time, Pallas kernels for 0%

profile of v5, /device:TPU:35, one launch (start us, length us, event | category | flops | bytes accessed | tf_op | source)
XLA Modules:
  0.0 122.4 jit_solution(9333146271174392633)
XLA Ops:
  0.0 1.3 %copy.29.pairs_ref = s32[4,2]{1,0:T(4,128)} copy(s32[4,2]{0,1:T(2,128)} %param.7) | data formatting | bytes 64 | tf_op args[2]
  1.4 2.8 %shard_map.37 = (bf16[16,8,1152]{2,1,0:T(8,128)(2,1)}, bf16[16,8,1152]{2,1,0:T(8,128)(2,1)}) custom-call(s32[4,2]{1,0:T(4,128)} %copy.29.pairs_ref, bf16[128,1024]{1,0:T(8,128)(2,1)} %traces_ref.1, s32[1,128]{1,0:T(1,128)} %bitcast.29), custom_call_target="tpu_custom_call" | custom-call | tf_op jit(solution)/shard_map/pallas_call | solution.py:96
  4.2 15.2 %all_to_all.20 = bf16[16,8,1152]{2,1,0:T(8,128)(2,1)S(1)} all-to-all(bf16[16,8,1152]{2,1,0:T(8,128)(2,1)} %get-tuple-element.9), channel_id=1, replica_groups=mesh['row'=16,'col'=16] {'row'}, dimensions={0} | all-to-all | bytes 589824 | tf_op jit(solution)/shard_map/all_to_all | solution.py:117
  19.3 11.2 %all-to-all-start = ((bf16[16,8,1152]{2,1,0:T(8,128)(2,1)}), bf16[16,8,1152]{2,1,0:T(8,128)(2,1)S(1)}, u32[]{:S(2)}, u32[]{:S(2)}) async-start(bf16[16,8,1152]{2,1,0:T(8,128)(2,1)} %get-tuple-element.8), calls=%async_computation | async-start | bytes 589824 | tf_op jit(solution)/shard_map/all_to_all | solution.py:117
  30.5 0.1 copy.34
  30.6 0.1 copy.35
  30.7 0.1 copy.36
  30.8 0.1 reshape.52
  30.9 0.6 gather_fusion.1
  31.6 1.1 broadcast_select_fusion
  32.7 12.3 %all-to-all-done = bf16[16,8,1152]{2,1,0:T(8,128)(2,1)S(1)} async-done(((bf16[16,8,1152]{2,1,0:T(8,128)(2,1)}), bf16[16,8,1152]{2,1,0:T(8,128)(2,1)S(1)}, u32[]{:S(2)}, u32[]{:S(2)}) %all-to-all-start) | async-done | bytes 294944 | tf_op jit(solution)/shard_map/all_to_all | solution.py:117
  45.0 5.1 %all-to-all-start.3 = ((bf16[16,4,8,1024]{3,2,1,0:T(8,128)(2,1)}), bf16[16,4,8,1024]{3,2,1,0:T(8,128)(2,1)S(1)}, u32[]{:S(2)}, u32[]{:S(2)}) async-start(bf16[16,4,8,1024]{3,2,1,0:T(8,128)(2,1)} %broadcast_select_fusion), calls=%async_computation.3 | async-start | bytes 2097152 | tf_op jit(solution)/shard_map/all_to_all | solution.py:120
  50.1 0.1 copy.30
  50.2 0.1 copy.31
  50.3 0.1 copy.32
  50.4 0.1 reshape.48
  50.5 0.6 gather_fusion
  51.1 0.0 copy-start
  51.2 1.1 broadcast_select_fusion.1
  52.3 21.4 %all-to-all-done.3 = bf16[16,4,8,1024]{3,2,1,0:T(8,128)(2,1)S(1)} async-done(((bf16[16,4,8,1024]{3,2,1,0:T(8,128)(2,1)}), bf16[16,4,8,1024]{3,2,1,0:T(8,128)(2,1)S(1)}, u32[]{:S(2)}, u32[]{:S(2)}) %all-to-all-start.3) | async-done | bytes 1048608 | tf_op jit(solution)/shard_map/all_to_all | solution.py:120
  73.7 5.5 %all-to-all-start.1 = ((bf16[16,4,8,1024]{3,2,1,0:T(8,128)(2,1)}), bf16[16,4,8,1024]{3,2,1,0:T(8,128)(2,1)S(1)}, u32[]{:S(2)}, u32[]{:S(2)}) async-start(bf16[16,4,8,1024]{3,2,1,0:T(8,128)(2,1)} %broadcast_select_fusion.1), calls=%async_computation.1 | async-start | bytes 2097152 | tf_op jit(solution)/shard_map/all_to_all | solution.py:120
  79.3 0.0 copy-done
  79.3 0.1 copy.41
  79.4 1.3 %copy.38 = bf16[4,128,1024]{1,2,0:T(8,128)(2,1)} copy(bf16[4,128,1024]{2,1,0:T(8,128)(2,1)S(1)} %bitcast.28) | data formatting | bytes 2097152 | tf_op jit(solution)/shard_map/reshape | solution.py:121
  80.7 1.4 %convert_bitcast_fusion.r_ref = f32[4,1152,128]{2,1,0:T(8,128)S(1)} fusion(bf16[4,128,1024]{1,2,0:T(8,128)(2,1)} %copy.38), kind=kLoop, calls=%fused_computation.2 | loop fusion | flops 589824 | bytes 3407872 | tf_op jit(solution)/shard_map/convert_element_type | solution.py:49
  82.1 28.5 %all-to-all-done.1 = bf16[16,4,8,1024]{3,2,1,0:T(8,128)(2,1)S(1)} async-done(((bf16[16,4,8,1024]{3,2,1,0:T(8,128)(2,1)}), bf16[16,4,8,1024]{3,2,1,0:T(8,128)(2,1)S(1)}, u32[]{:S(2)}, u32[]{:S(2)}) %all-to-all-start.1) | async-done | bytes 1048608 | tf_op jit(solution)/shard_map/all_to_all | solution.py:120
  110.6 0.1 copy_bitcast_fusion.1.l_ref
  110.6 11.7 %shard_map.38 = bf16[4,65,128,128]{3,2,1,0:T(8,128)(2,1)} custom-call(s32[4]{0:T(128)S(1)} %fusion.live_ref, bf16[4,128,1024]{2,1,0:T(8,128)(2,1)S(1)} %copy_bitcast_fusion.1.l_ref, f32[4,1152,128]{2,1,0:T(8,128)S(1)} %convert_bitcast_fusion.r_ref), custom_call_target="tpu_custom_call" | custom-call | tf_op jit(solution)/shard_map/pallas_call | solution.py:50
  (11 shorter events, 0.1 us)
Async XLA Ops:
  19.3 25.7 %all-to-all-start = ((bf16[16,8,1152]{2,1,0:T(8,128)(2,1)}), bf16[16,8,1152]{2,1,0:T(8,128)(2,1)S(1)}, u32[]{:S(2)}, u32[]{:S(2)}) async-start(bf16[16,8,1152]{2,1,0:T(8,128)(2,1)} %get-tuple-element.8), calls=%async_computation | async-start | bytes 589824 | tf_op jit(solution)/shard_map/all_to_all | solution.py:117
  45.0 28.7 %all-to-all-start.3 = ((bf16[16,4,8,1024]{3,2,1,0:T(8,128)(2,1)}), bf16[16,4,8,1024]{3,2,1,0:T(8,128)(2,1)S(1)}, u32[]{:S(2)}, u32[]{:S(2)}) async-start(bf16[16,4,8,1024]{3,2,1,0:T(8,128)(2,1)} %broadcast_select_fusion), calls=%async_computation.3 | async-start | bytes 2097152 | tf_op jit(solution)/shard_map/all_to_all | solution.py:120
  51.1 28.1 %copy-start = (s32[4,2]{0,1:T(2,128)S(1)}, s32[4,2]{0,1:T(2,128)}, u32[]{:S(2)}) copy-start(s32[4,2]{0,1:T(2,128)} %param.7) | copy-start | bytes 100
  73.7 36.8 %all-to-all-start.1 = ((bf16[16,4,8,1024]{3,2,1,0:T(8,128)(2,1)}), bf16[16,4,8,1024]{3,2,1,0:T(8,128)(2,1)S(1)}, u32[]{:S(2)}, u32[]{:S(2)}) async-start(bf16[16,4,8,1024]{3,2,1,0:T(8,128)(2,1)} %broadcast_select_fusion.1), calls=%async_computation.1 | async-start | bytes 2097152 | tf_op jit(solution)/shard_map/all_to_all | solution.py:120

commit v6 on v5

--- a/solution.py
+++ b/solution.py
@@ -67,7 +67,7 @@
 def prepare_kernel(pairs_ref, traces_ref, alive_ref, col_ref, row_ref):
     pieces, piece, width = col_ref.shape
     length = traces_ref.shape[1]
-    slots = pairs_ref.shape[0]
+    slots = pairs_ref.shape[1]
     samples = traces_ref[...].astype(jnp.float32)
     centered = samples - jnp.mean(samples, axis=1, keepdims=True)
     power = jnp.mean(centered * centered, axis=1, keepdims=True)
@@ -80,8 +80,8 @@
     row_meta = jnp.zeros((piece, width - length), jnp.float32)
     for s in range(slots):
         at = (sublane == 0) & (lane == s)
-        col_meta = jnp.where(at, (jnp.maximum(pairs_ref[s, 0], 0) % pieces).astype(jnp.float32), col_meta)
-        row_meta = jnp.where(at, (jnp.maximum(pairs_ref[s, 1], 0) // pieces).astype(jnp.float32), row_meta)
+        col_meta = jnp.where(at, (jnp.maximum(pairs_ref[0, s], 0) % pieces).astype(jnp.float32), col_meta)
+        row_meta = jnp.where(at, (jnp.maximum(pairs_ref[1, s], 0) // pieces).astype(jnp.float32), row_meta)
     for p in range(pieces):
         rows = whitened[p * piece:(p + 1) * piece].astype(col_ref.dtype)
         col_ref[p, :, :length] = rows
@@ -108,7 +108,7 @@
             ],
         ),
         out_shape=[shape, shape],
-    )(pair_list, traces, alive.reshape(1, channels))
+    )(pair_list.T, traces, alive.reshape(1, channels))
 
 
 def fetch_blocks(pieces, axis, slots):

time: 124 us -> 122 us (0.984)
  local copies, waits for them, and re-layouts: 4.81 us -> 3.46 us
    unnamed x3 -> x2, local copies, waits for them, and re-layouts: 1.36 us -> 0.01 us
where the time goes in v6:
time: 122 us; the launch traced here: 121 us
  waiting for transfers between devices  62.3 us (51%)
  starting transfers between devices  21.8 us (18%)
  blocking collectives  15.2 us (12%)
  Pallas kernels  14.5 us (12%)
  other arithmetic  3.71 us (3%)
  local copies, waits for them, and re-layouts  3.46 us (3%)
    all_to_all x2, waiting for transfers between devices, fetch_blocks(): arrived = lax.all_to_all(chosen, axis, 0, 0, tiled=True)  49.9 us
    all_to_all x1, blocking collectives, fetch_blocks(): spread = lax.all_to_all(pieces, axis, 0, 0, tiled=True)  15.2 us
    all_to_all x1, waiting for transfers between devices, fetch_blocks(): spread = lax.all_to_all(pieces, axis, 0, 0, tiled=True)  12.3 us
    pallas_call x1, Pallas kernels, correlate_all(): pl.pallas_call(correlate_kernel, grid_spec=pltpu.PrefetchScalarGridSpec(n...  11.7 us
    all_to_all x1, starting transfers between devices, fetch_blocks(): spread = lax.all_to_all(pieces, axis, 0, 0, tiled=True)  11.2 us
    all_to_all x2, starting transfers between devices, fetch_blocks(): arrived = lax.all_to_all(chosen, axis, 0, 0, tiled=True)  10.6 us
    pallas_call x1, Pallas kernels, prepare(): pl.pallas_call(prepare_kernel, grid_spec=pltpu.PrefetchScalarGridSpec(num...  2.8 us
  transfers between devices with their start and end apart: 3, of which 3 were waited for; matrix products, arithmetic and copies ran while one was open for 6% of the time, Pallas kernels for 0%

profile of v6, /device:TPU:35, one launch (start us, length us, event | category | flops | bytes accessed | tf_op | source)
XLA Modules:
  0.0 121.0 jit_solution(488478098406773858)
XLA Ops:
  0.0 2.8 %shard_map.37 = (bf16[16,8,1152]{2,1,0:T(8,128)(2,1)}, bf16[16,8,1152]{2,1,0:T(8,128)(2,1)}) custom-call(s32[2,4]{1,0:T(2,128)} %bitcast.30, bf16[128,1024]{1,0:T(8,128)(2,1)} %traces_ref.1, s32[1,128]{1,0:T(1,128)} %bitcast.31), custom_call_target="tpu_custom_call" | custom-call | tf_op jit(solution)/shard_map/pallas_call | solution.py:96
  2.8 15.2 %all_to_all.20 = bf16[16,8,1152]{2,1,0:T(8,128)(2,1)S(1)} all-to-all(bf16[16,8,1152]{2,1,0:T(8,128)(2,1)} %get-tuple-element.9), channel_id=1, replica_groups=mesh['row'=16,'col'=16] {'row'}, dimensions={0} | all-to-all | bytes 589824 | tf_op jit(solution)/shard_map/all_to_all | solution.py:117
  18.0 11.2 %all-to-all-start = ((bf16[16,8,1152]{2,1,0:T(8,128)(2,1)}), bf16[16,8,1152]{2,1,0:T(8,128)(2,1)S(1)}, u32[]{:S(2)}, u32[]{:S(2)}) async-start(bf16[16,8,1152]{2,1,0:T(8,128)(2,1)} %get-tuple-element.8), calls=%async_computation | async-start | bytes 589824 | tf_op jit(solution)/shard_map/all_to_all | solution.py:117
  29.2 0.1 copy.30
  29.3 0.1 copy.31
  29.4 0.1 copy.32
  29.4 0.1 reshape.52
  29.6 0.6 gather_fusion.1
  30.2 1.1 broadcast_select_fusion
  31.3 12.3 %all-to-all-done = bf16[16,8,1152]{2,1,0:T(8,128)(2,1)S(1)} async-done(((bf16[16,8,1152]{2,1,0:T(8,128)(2,1)}), bf16[16,8,1152]{2,1,0:T(8,128)(2,1)S(1)}, u32[]{:S(2)}, u32[]{:S(2)}) %all-to-all-start) | async-done | bytes 294944 | tf_op jit(solution)/shard_map/all_to_all | solution.py:117
  43.7 5.1 %all-to-all-start.3 = ((bf16[16,4,8,1024]{3,2,1,0:T(8,128)(2,1)}), bf16[16,4,8,1024]{3,2,1,0:T(8,128)(2,1)S(1)}, u32[]{:S(2)}, u32[]{:S(2)}) async-start(bf16[16,4,8,1024]{3,2,1,0:T(8,128)(2,1)} %broadcast_select_fusion), calls=%async_computation.3 | async-start | bytes 2097152 | tf_op jit(solution)/shard_map/all_to_all | solution.py:120
  48.8 0.1 copy.26
  48.8 0.1 copy.27
  48.9 0.1 copy.28
  49.0 0.1 reshape.48
  49.2 0.6 gather_fusion
  49.8 0.0 copy-start
  49.8 1.1 broadcast_select_fusion.1
  50.9 21.4 %all-to-all-done.3 = bf16[16,4,8,1024]{3,2,1,0:T(8,128)(2,1)S(1)} async-done(((bf16[16,4,8,1024]{3,2,1,0:T(8,128)(2,1)}), bf16[16,4,8,1024]{3,2,1,0:T(8,128)(2,1)S(1)}, u32[]{:S(2)}, u32[]{:S(2)}) %all-to-all-start.3) | async-done | bytes 1048608 | tf_op jit(solution)/shard_map/all_to_all | solution.py:120
  72.4 5.5 %all-to-all-start.1 = ((bf16[16,4,8,1024]{3,2,1,0:T(8,128)(2,1)}), bf16[16,4,8,1024]{3,2,1,0:T(8,128)(2,1)S(1)}, u32[]{:S(2)}, u32[]{:S(2)}) async-start(bf16[16,4,8,1024]{3,2,1,0:T(8,128)(2,1)} %broadcast_select_fusion.1), calls=%async_computation.1 | async-start | bytes 2097152 | tf_op jit(solution)/shard_map/all_to_all | solution.py:120
  77.9 0.0 copy-done
  77.9 0.1 copy.37
  78.0 1.3 %copy.34 = bf16[4,128,1024]{1,2,0:T(8,128)(2,1)} copy(bf16[4,128,1024]{2,1,0:T(8,128)(2,1)S(1)} %bitcast.29) | data formatting | bytes 2097152 | tf_op jit(solution)/shard_map/reshape | solution.py:121
  79.3 1.4 %convert_bitcast_fusion.r_ref = f32[4,1152,128]{2,1,0:T(8,128)S(1)} fusion(bf16[4,128,1024]{1,2,0:T(8,128)(2,1)} %copy.34), kind=kLoop, calls=%fused_computation.2 | loop fusion | flops 589824 | bytes 3407872 | tf_op jit(solution)/shard_map/convert_element_type | solution.py:49
  80.7 28.5 %all-to-all-done.1 = bf16[16,4,8,1024]{3,2,1,0:T(8,128)(2,1)S(1)} async-done(((bf16[16,4,8,1024]{3,2,1,0:T(8,128)(2,1)}), bf16[16,4,8,1024]{3,2,1,0:T(8,128)(2,1)S(1)}, u32[]{:S(2)}, u32[]{:S(2)}) %all-to-all-start.1) | async-done | bytes 1048608 | tf_op jit(solution)/shard_map/all_to_all | solution.py:120
  109.2 0.1 copy_bitcast_fusion.1.l_ref
  109.3 11.7 %shard_map.38 = bf16[4,65,128,128]{3,2,1,0:T(8,128)(2,1)} custom-call(s32[4]{0:T(128)S(1)} %fusion.live_ref, bf16[4,128,1024]{2,1,0:T(8,128)(2,1)S(1)} %copy_bitcast_fusion.1.l_ref, f32[4,1152,128]{2,1,0:T(8,128)S(1)} %convert_bitcast_fusion.r_ref), custom_call_target="tpu_custom_call" | custom-call | tf_op jit(solution)/shard_map/pallas_call | solution.py:50
  (11 shorter events, 0.1 us)
Async XLA Ops:
  18.0 25.7 %all-to-all-start = ((bf16[16,8,1152]{2,1,0:T(8,128)(2,1)}), bf16[16,8,1152]{2,1,0:T(8,128)(2,1)S(1)}, u32[]{:S(2)}, u32[]{:S(2)}) async-start(bf16[16,8,1152]{2,1,0:T(8,128)(2,1)} %get-tuple-element.8), calls=%async_computation | async-start | bytes 589824 | tf_op jit(solution)/shard_map/all_to_all | solution.py:117
  43.7 28.7 %all-to-all-start.3 = ((bf16[16,4,8,1024]{3,2,1,0:T(8,128)(2,1)}), bf16[16,4,8,1024]{3,2,1,0:T(8,128)(2,1)S(1)}, u32[]{:S(2)}, u32[]{:S(2)}) async-start(bf16[16,4,8,1024]{3,2,1,0:T(8,128)(2,1)} %broadcast_select_fusion), calls=%async_computation.3 | async-start | bytes 2097152 | tf_op jit(solution)/shard_map/all_to_all | solution.py:120
  49.8 28.1 %copy-start = (s32[4,2]{0,1:T(2,128)S(1)}, s32[4,2]{0,1:T(2,128)}, u32[]{:S(2)}) copy-start(s32[4,2]{0,1:T(2,128)} %param.7) | copy-start | bytes 100
  72.4 36.8 %all-to-all-start.1 = ((bf16[16,4,8,1024]{3,2,1,0:T(8,128)(2,1)}), bf16[16,4,8,1024]{3,2,1,0:T(8,128)(2,1)S(1)}, u32[]{:S(2)}, u32[]{:S(2)}) async-start(bf16[16,4,8,1024]{3,2,1,0:T(8,128)(2,1)} %broadcast_select_fusion.1), calls=%async_computation.1 | async-start | bytes 2097152 | tf_op jit(solution)/shard_map/all_to_all | solution.py:120

commit v7 on v6

--- a/solution.py
+++ b/solution.py
@@ -31,7 +31,7 @@
         for first in range(0, LAGS, PAIR):
             lags = range(first, min(first + PAIR, LAGS))
             shifted = jnp.concatenate(
-                [r_ref[0, pl.ds(PAD - REACH + k, length), :].astype(jnp.bfloat16) for k in lags], axis=1
+                [r_ref[0, pl.ds(PAD - REACH + k, length), :] for k in lags], axis=1
             )
             summed = jnp.dot(left, shifted, preferred_element_type=jnp.float32)
             summed = (summed * (1.0 / length)).astype(o_ref.dtype)
@@ -46,7 +46,7 @@
 def correlate_all(live, left, right):
     slots, width, length = left.shape
     padded = jnp.pad(right, ((0, 0), (0, 0), (PAD, PAD)))
-    padded = jnp.transpose(padded, (0, 2, 1)).astype(jnp.float32)
+    padded = jnp.transpose(padded, (0, 2, 1))
     out = pl.pallas_call(
         correlate_kernel,
         grid_spec=pltpu.PrefetchScalarGridSpec(

time: 122 us -> 122 us (level)
  waiting for transfers between devices: 62.3 us -> 64.2 us
  other arithmetic: 3.71 us -> 2.33 us
    all_to_all x2, waiting for transfers between devices: 49.9 us -> 51.8 us  [fetch_blocks(): arrived = lax.all_to_all(chosen, axis, 0, 0, tiled=True)]
    convert_element_type x1 -> x0, other arithmetic: 1.38 us -> none  [correlate_all(): padded = jnp.transpose(padded, (0, 2, 1)).astype(jnp.float32)]
  transfers between devices with their start and end apart: 3 -> 3, of which waited for: 3 -> 3; matrix products, arithmetic and copies ran while one was open for 6% -> 4% of each run, Pallas kernels for 0% -> 0%
where the time goes in v7:
time: 122 us; the launch traced here: 121 us
  waiting for transfers between devices  64.2 us (53%)
  starting transfers between devices  21.8 us (18%)
  blocking collectives  15.2 us (12%)
  Pallas kernels  14.6 us (12%)
  local copies, waits for them, and re-layouts  2.92 us (2%)
  other arithmetic  2.33 us (2%)
    all_to_all x2, waiting for transfers between devices, fetch_blocks(): arrived = lax.all_to_all(chosen, axis, 0, 0, tiled=True)  51.8 us
    all_to_all x1, blocking collectives, fetch_blocks(): spread = lax.all_to_all(pieces, axis, 0, 0, tiled=True)  15.2 us
    all_to_all x1, waiting for transfers between devices, fetch_blocks(): spread = lax.all_to_all(pieces, axis, 0, 0, tiled=True)  12.3 us
    pallas_call x1, Pallas kernels, correlate_all(): pl.pallas_call(correlate_kernel, grid_spec=pltpu.PrefetchScalarGridSpec(n...  11.8 us
    all_to_all x1, starting transfers between devices, fetch_blocks(): spread = lax.all_to_all(pieces, axis, 0, 0, tiled=True)  11.2 us
    all_to_all x2, starting transfers between devices, fetch_blocks(): arrived = lax.all_to_all(chosen, axis, 0, 0, tiled=True)  10.6 us
    pallas_call x1, Pallas kernels, prepare(): pl.pallas_call(prepare_kernel, grid_spec=pltpu.PrefetchScalarGridSpec(num...  2.8 us
  transfers between devices with their start and end apart: 3, of which 3 were waited for; matrix products, arithmetic and copies ran while one was open for 4% of the time, Pallas kernels for 0%

profile of v7, /device:TPU:35, one launch (start us, length us, event | category | flops | bytes accessed | tf_op | source)
XLA Modules:
  0.0 121.1 jit_solution(7474046012586379025)
XLA Ops:
  0.0 2.8 %shard_map.37 = (bf16[16,8,1152]{2,1,0:T(8,128)(2,1)}, bf16[16,8,1152]{2,1,0:T(8,128)(2,1)}) custom-call(s32[2,4]{1,0:T(2,128)} %bitcast.30, bf16[128,1024]{1,0:T(8,128)(2,1)} %traces_ref.1, s32[1,128]{1,0:T(1,128)} %bitcast.31), custom_call_target="tpu_custom_call" | custom-call | tf_op jit(solution)/shard_map/pallas_call | solution.py:96
  2.8 15.2 %all_to_all.20 = bf16[16,8,1152]{2,1,0:T(8,128)(2,1)S(1)} all-to-all(bf16[16,8,1152]{2,1,0:T(8,128)(2,1)} %get-tuple-element.9), channel_id=1, replica_groups=mesh['row'=16,'col'=16] {'row'}, dimensions={0} | all-to-all | bytes 589824 | tf_op jit(solution)/shard_map/all_to_all | solution.py:117
  18.0 11.2 %all-to-all-start = ((bf16[16,8,1152]{2,1,0:T(8,128)(2,1)}), bf16[16,8,1152]{2,1,0:T(8,128)(2,1)S(1)}, u32[]{:S(2)}, u32[]{:S(2)}) async-start(bf16[16,8,1152]{2,1,0:T(8,128)(2,1)} %get-tuple-element.8), calls=%async_computation | async-start | bytes 589824 | tf_op jit(solution)/shard_map/all_to_all | solution.py:117
  29.2 0.1 copy.30
  29.3 0.1 copy.31
  29.4 0.1 copy.32
  29.4 0.1 reshape.52
  29.6 0.6 gather_fusion.1
  30.2 1.1 broadcast_select_fusion
  31.3 12.3 %all-to-all-done = bf16[16,8,1152]{2,1,0:T(8,128)(2,1)S(1)} async-done(((bf16[16,8,1152]{2,1,0:T(8,128)(2,1)}), bf16[16,8,1152]{2,1,0:T(8,128)(2,1)S(1)}, u32[]{:S(2)}, u32[]{:S(2)}) %all-to-all-start) | async-done | bytes 294944 | tf_op jit(solution)/shard_map/all_to_all | solution.py:117
  43.7 5.1 %all-to-all-start.3 = ((bf16[16,4,8,1024]{3,2,1,0:T(8,128)(2,1)}), bf16[16,4,8,1024]{3,2,1,0:T(8,128)(2,1)S(1)}, u32[]{:S(2)}, u32[]{:S(2)}) async-start(bf16[16,4,8,1024]{3,2,1,0:T(8,128)(2,1)} %broadcast_select_fusion), calls=%async_computation.3 | async-start | bytes 2097152 | tf_op jit(solution)/shard_map/all_to_all | solution.py:120
  48.8 0.1 copy.26
  48.8 0.1 copy.27
  48.9 0.1 copy.28
  49.0 0.1 reshape.48
  49.2 0.6 gather_fusion
  49.8 1.1 broadcast_select_fusion.1
  50.9 0.0 copy-start
  50.9 21.4 %all-to-all-done.3 = bf16[16,4,8,1024]{3,2,1,0:T(8,128)(2,1)S(1)} async-done(((bf16[16,4,8,1024]{3,2,1,0:T(8,128)(2,1)}), bf16[16,4,8,1024]{3,2,1,0:T(8,128)(2,1)S(1)}, u32[]{:S(2)}, u32[]{:S(2)}) %all-to-all-start.3) | async-done | bytes 1048608 | tf_op jit(solution)/shard_map/all_to_all | solution.py:120
  72.4 5.5 %all-to-all-start.1 = ((bf16[16,4,8,1024]{3,2,1,0:T(8,128)(2,1)}), bf16[16,4,8,1024]{3,2,1,0:T(8,128)(2,1)S(1)}, u32[]{:S(2)}, u32[]{:S(2)}) async-start(bf16[16,4,8,1024]{3,2,1,0:T(8,128)(2,1)} %broadcast_select_fusion.1), calls=%async_computation.1 | async-start | bytes 2097152 | tf_op jit(solution)/shard_map/all_to_all | solution.py:120
  77.9 0.0 copy-done
  77.9 0.1 copy.37
  78.0 0.7 copy.34
  78.7 0.1 pad_bitcast_fusion.r_ref
  78.8 30.4 %all-to-all-done.1 = bf16[16,4,8,1024]{3,2,1,0:T(8,128)(2,1)S(1)} async-done(((bf16[16,4,8,1024]{3,2,1,0:T(8,128)(2,1)}), bf16[16,4,8,1024]{3,2,1,0:T(8,128)(2,1)S(1)}, u32[]{:S(2)}, u32[]{:S(2)}) %all-to-all-start.1) | async-done | bytes 1048608 | tf_op jit(solution)/shard_map/all_to_all | solution.py:120
  109.2 0.1 copy_bitcast_fusion.1.l_ref
  109.3 11.8 %shard_map.38 = bf16[4,65,128,128]{3,2,1,0:T(8,128)(2,1)} custom-call(s32[4]{0:T(128)S(1)} %fusion.live_ref, bf16[4,128,1024]{2,1,0:T(8,128)(2,1)S(1)} %copy_bitcast_fusion.1.l_ref, bf16[4,1152,128]{2,1,0:T(8,128)(2,1)S(1)} %pad_bitcast_fusion.r_ref), custom_call_target="tpu_custom_call" | custom-call | tf_op jit(solution)/shard_map/pallas_call | solution.py:50
  (11 shorter events, 0.1 us)
Async XLA Ops:
  18.0 25.7 %all-to-all-start = ((bf16[16,8,1152]{2,1,0:T(8,128)(2,1)}), bf16[16,8,1152]{2,1,0:T(8,128)(2,1)S(1)}, u32[]{:S(2)}, u32[]{:S(2)}) async-start(bf16[16,8,1152]{2,1,0:T(8,128)(2,1)} %get-tuple-element.8), calls=%async_computation | async-start | bytes 589824 | tf_op jit(solution)/shard_map/all_to_all | solution.py:117
  43.7 28.7 %all-to-all-start.3 = ((bf16[16,4,8,1024]{3,2,1,0:T(8,128)(2,1)}), bf16[16,4,8,1024]{3,2,1,0:T(8,128)(2,1)S(1)}, u32[]{:S(2)}, u32[]{:S(2)}) async-start(bf16[16,4,8,1024]{3,2,1,0:T(8,128)(2,1)} %broadcast_select_fusion), calls=%async_computation.3 | async-start | bytes 2097152 | tf_op jit(solution)/shard_map/all_to_all | solution.py:120
  50.9 27.0 %copy-start = (s32[4,2]{0,1:T(2,128)S(1)}, s32[4,2]{0,1:T(2,128)}, u32[]{:S(2)}) copy-start(s32[4,2]{0,1:T(2,128)} %param.7) | copy-start | bytes 100
  72.4 36.8 %all-to-all-start.1 = ((bf16[16,4,8,1024]{3,2,1,0:T(8,128)(2,1)}), bf16[16,4,8,1024]{3,2,1,0:T(8,128)(2,1)S(1)}, u32[]{:S(2)}, u32[]{:S(2)}) async-start(bf16[16,4,8,1024]{3,2,1,0:T(8,128)(2,1)} %broadcast_select_fusion.1), calls=%async_computation.1 | async-start | bytes 2097152 | tf_op jit(solution)/shard_map/all_to_all | solution.py:120
